TPU v7x, 512 devices: a whole 4x8x8 slice. The times are simulated.
512 devices in a mesh: req: 64 (over x, y, core), tp: 8 (over z).
Axes of the slice: x: 4, y: 8, z: 8, core: 2. Of those that a mesh axis runs over, the one named last changes fastest.
Arguments:
- vit_context: bfloat16 [32768, 4096], P('req', 'tp'), may hold values from -6 to 6
- vision_residual: bfloat16 [32768, 4096], P('req', 'tp'), may hold values from -75 to 75
- out_weight: bfloat16 [4096, 4096], P('tp', 'req'), may hold values from -0.09375 to 0.09375
- layer_scale: float32 [4096], P('tp'), may hold values from 0.2 to 2
- prompt: bfloat16 [64, 256, 4096], P('req', None, 'tp'), may hold values from -75 to 75
- prompt_len: int32 [64], P('req'), may hold values from 128 to 256
- image_at: int32 [64], P('req'), may hold values from 0 to 128
- grid_sizes: int32 [128, 2], replicated, may hold values from 7 to 8, as said below
- image_owner: int32 [128], replicated, may hold values from 0 to 63, as said below
- norm_gain: float32 [4096], replicated, may hold values from 0.5 to 1.5
- qkv_weight: bfloat16 [4096, 6144], P('req', 'tp'), may hold values from -0.09375 to 0.09375
Outputs:
- qkv: bfloat16 [24576, 6144], P('req', 'tp')
Inputs may be any that keep to these rules, and one draw needn't show every extreme that they name: `image_owner`: each request owns exactly 2 images. `grid_sizes`: each side is 7 or 8; in every draw the images of some request are all 8 by 8, so that request has exactly 128 merged rows.
All inputs are finite; a program needn't handle non-finite values.
Results may differ from a plain program's by a relative error of at most 0.008.
Values may be sent and summed in bfloat16 or wider, within the bound.
No kernel may reach another device: no remote copies, remote signals or barrier semaphores. Data moves between devices by JAX's collectives and lax.ppermute only.
A program may use at most 64 MiB of HBM per device.

v0:
```python
import jax
import jax.numpy as jnp
from jax import lax
from jax.sharding import PartitionSpec as P

HEAD = 128
GROUP = 4
IMG_MAX = 128


def request_plan(grid_sizes, image_owner, requests):
    image_rows = grid_sizes[:, 0] * grid_sizes[:, 1]
    member = (image_owner[:, None] == jnp.arange(requests, dtype=jnp.int32)[None, :]).astype(
        jnp.int32
    )
    counts = jnp.sum(image_rows[:, None] * member, axis=0)
    starts = jnp.cumsum(counts) - counts
    return (counts, starts)


def rope_tables(count):
    half_size = HEAD // 2
    exponent = jnp.arange(half_size, dtype=jnp.float32) * (2.0 / HEAD)
    frequency = jnp.exp(-exponent * jnp.log(jnp.float32(500000.0)))
    angles = jnp.arange(count, dtype=jnp.float32)[:, None] * frequency[None, :]
    return (jnp.cos(angles), jnp.sin(angles))


def apply_rope(projected, cosine_table, sine_table):
    seq_rows = projected.shape[0]
    head_blocks = projected.reshape(seq_rows, -1, GROUP + 2, HEAD)
    turning = head_blocks[:, :, : GROUP + 1, :]
    first_half = turning[..., : HEAD // 2]
    second_half = turning[..., HEAD // 2 :]
    cosine_wide = cosine_table[:, None, None, :]
    sine_wide = sine_table[:, None, None, :]
    turned = jnp.concatenate(
        [
            first_half * cosine_wide - second_half * sine_wide,
            second_half * cosine_wide + first_half * sine_wide,
        ],
        axis=-1,
    )
    head_blocks = jnp.concatenate([turned, head_blocks[:, :, GROUP + 1 :, :]], axis=2)
    return head_blocks.reshape(seq_rows, -1)


def normalize(embedded, norm_gain):
    values = embedded.astype(jnp.float32)
    mean_square = jnp.mean(values * values, axis=-1, keepdims=True)
    return (values * lax.rsqrt(mean_square + 1e-05) * norm_gain[None, :]).astype(jnp.bfloat16)


def shards(
    vit_context,
    vision_residual,
    out_weight,
    layer_scale,
    prompt,
    prompt_len,
    image_at,
    grid_sizes,
    image_owner,
    norm_gain,
    qkv_weight,
):
    requests = lax.axis_size("req")
    device_index = lax.axis_index("req")
    feature_width = vit_context.shape[1]
    merged_context = jnp.mean(
        vit_context.astype(jnp.float32).reshape(-1, 4, feature_width), axis=1
    ).astype(jnp.bfloat16)
    merged_residual = jnp.mean(
        vision_residual.astype(jnp.float32).reshape(-1, 4, feature_width), axis=1
    )
    partial_value = jnp.dot(
        merged_context,
        lax.all_gather(out_weight, "req", axis=1, tiled=True),
        preferred_element_type=jnp.float32,
    )
    summed = lax.psum(partial_value.astype(jnp.bfloat16), "tp").astype(jnp.float32)
    own_share = lax.dynamic_slice_in_dim(
        summed, lax.axis_index("tp") * feature_width, feature_width, 1
    )
    merged = (merged_residual + layer_scale[None, :] * own_share).astype(jnp.bfloat16)
    merged_count = merged.shape[0]
    counts, starts = request_plan(grid_sizes, image_owner, requests)
    request_ends = starts + counts
    capacity = (IMG_MAX + requests - 1) // requests
    request_ids = jnp.arange(requests, dtype=jnp.int32)
    group_index = jnp.arange(merged_count, dtype=jnp.int32) * requests + device_index
    destination = jnp.sum((request_ends[None, :] <= group_index[:, None]).astype(jnp.int32), axis=1)
    owned_start = jnp.sum(
        jnp.where(destination[:, None] == request_ids[None, :], starts[None, :], 0), axis=1
    )
    target = destination * capacity + (group_index - owned_start) // requests
    usable = destination < requests
    send_slots = jnp.arange(requests * capacity, dtype=jnp.int32)
    placing = ((send_slots[:, None] == target[None, :]) & usable[None, :]).astype(jnp.bfloat16)
    outgoing = jnp.dot(placing, merged, preferred_element_type=jnp.float32).astype(jnp.bfloat16)
    arrived = lax.all_to_all(
        outgoing.reshape(requests, capacity, feature_width),
        "req",
        split_axis=0,
        concat_axis=0,
        tiled=True,
    )
    arrived = arrived.reshape(requests * capacity, feature_width)
    own_request = request_ids == device_index
    own_count = jnp.sum(jnp.where(own_request, counts, 0))
    own_start = jnp.sum(jnp.where(own_request, starts, 0))
    image_from = image_at[0]
    prompt_count = prompt_len[0]
    seq_slots = prompt.shape[1] + IMG_MAX
    slot_index = jnp.arange(seq_slots, dtype=jnp.int32)
    image_row = slot_index - image_from
    in_image = (image_row >= 0) & (image_row < own_count)
    is_live = slot_index < prompt_count + own_count
    from_prompt = is_live & jnp.logical_not(in_image)
    flat_index = (own_start + image_row) % requests * capacity + image_row // requests
    image_pick = ((flat_index[:, None] == send_slots[None, :]) & in_image[:, None]).astype(
        jnp.bfloat16
    )
    prompt_row = jnp.where(slot_index < image_from, slot_index, slot_index - own_count)
    prompt_ids = jnp.arange(prompt.shape[1], dtype=jnp.int32)
    prompt_pick = ((prompt_row[:, None] == prompt_ids[None, :]) & from_prompt[:, None]).astype(
        jnp.bfloat16
    )
    embedded = (
        jnp.dot(image_pick, arrived, preferred_element_type=jnp.float32)
        + jnp.dot(prompt_pick, prompt[0], preferred_element_type=jnp.float32)
    ).astype(jnp.bfloat16)
    gathered = lax.all_gather(embedded, "tp", axis=1, tiled=True)
    normed = normalize(gathered, norm_gain)
    projected = jnp.dot(
        normed,
        lax.all_gather(qkv_weight, "req", axis=0, tiled=True),
        preferred_element_type=jnp.float32,
    )
    cosine_table, sine_table = rope_tables(seq_slots)
    return apply_rope(projected, cosine_table, sine_table).astype(jnp.bfloat16)


def solution(mesh):
    in_specs = (
        P("req", "tp"),
        P("req", "tp"),
        P("tp", "req"),
        P("tp"),
        P("req", None, "tp"),
        P("req"),
        P("req"),
        P(),
        P(),
        P(),
        P("req", "tp"),
    )
    out_specs = P("req", "tp")
    return jax.shard_map(shards, mesh=mesh, in_specs=in_specs, out_specs=out_specs, check_vma=False)
```

profile of v0, /device:TPU:1, one launch (start us, length us, event | category | flops | bytes accessed | tf_op | source)
XLA Modules:
  0.0 352.9 jit_solution(7770393168710454331)
XLA Ops:
  6.5 0.7 all-gather.4.cloned.1.call-update
  7.3 1.4 reshape.205
  8.7 0.6 reduce_sum.78
  9.3 0.8 multiply_bitcast_fusion
  10.1 91.0 %all-gather.4.cloned.1.call-done = bf16[512,4096]{0,1:T(8,128)(2,1)} async-done(((bf16[512,64]{0,1:T(8,128)(2,1)}), bf16[512,4096]{0,1:T(8,128)(2,1)}) %all-gather.4.cloned.1.call-update) | async-done | bytes 4194320 | tf_op jit(solution)/shard_map/all_gather | solution.py:78
  101.1 4.6 %convolution_convert_fusion = bf16[128,4096]{1,0:T(8,128)(2,1)} fusion(bf16[512,4096]{0,1:T(8,128)(2,1)} %all-gather.4.cloned.1.call-done, f32[128,512]{1,0:T(8,128)S(1)} %reduce_sum.78), kind=kOutput, calls=%fused_computation.5 | convolution fusion | flops 537526272 | bytes 5505024 | tf_op jit(solution)/shard_map/dot_general | solution.py:76
  106.2 0.3 reshape.203
  106.5 0.6 reduce_sum.77
  107.3 0.7 fusion.38
  108.1 73.3 %all-reduce.2.cloned.1.call-done = bf16[128,4096]{1,0:T(8,128)(2,1)} async-done(((bf16[128,4096]{1,0:T(8,128)(2,1)}), bf16[128,4096]{1,0:T(8,128)(2,1)}) %all-reduce.2.cloned.1.call-update) | async-done | bytes 1048592 | tf_op jit(solution)/shard_map/psum | solution.py:81
  181.4 1.1 convolution_convert_fusion.1
  182.5 0.7 reshape.199
  183.3 14.2 %all-to-all-start = ((bf16[64,2,512]{2,1,0:T(2,128)(2,1)}), bf16[64,2,512]{2,1,0:T(2,128)(2,1)S(1)}, u32[]{:S(2)}, u32[]{:S(2)}) async-start(bf16[64,2,512]{2,1,0:T(2,128)(2,1)} %reshape.199), calls=%async_computation | async-start | bytes 262144 | tf_op jit(solution)/shard_map/all_to_all | solution.py:101
  199.3 0.6 fusion.37
  199.9 1.3 fusion.30
  201.2 6.6 %all-to-all-done = bf16[64,2,512]{2,1,0:T(2,128)(2,1)S(1)} async-done(((bf16[64,2,512]{2,1,0:T(2,128)(2,1)}), bf16[64,2,512]{2,1,0:T(2,128)(2,1)S(1)}, u32[]{:S(2)}, u32[]{:S(2)}) %all-to-all-start) | async-done | bytes 131104 | tf_op jit(solution)/shard_map/all_to_all | solution.py:101
  208.2 1.1 fusion.7
  209.3 0.5 all-gather.8.cloned.1.call-update
  209.9 0.4 fusion.21
  210.3 40.0 %all-gather.6.cloned.1.call-done = bf16[384,4096]{1,0:T(8,128)(2,1)} async-done(((bf16[384,512]{1,0:T(8,128)(2,1)}), bf16[384,4096]{1,0:T(8,128)(2,1)}) %all-gather.6.cloned.1.call-update) | async-done | bytes 3145744 | tf_op jit(solution)/shard_map/all_gather | solution.py:133
  250.3 2.6 fusion
  252.9 85.4 %all-gather.8.cloned.1.call-done = bf16[4096,768]{1,0:T(8,128)(2,1)} async-done(((bf16[64,768]{1,0:T(8,128)(2,1)}), bf16[4096,768]{1,0:T(8,128)(2,1)}) %all-gather.8.cloned.1.call-update) | async-done | bytes 6291472 | tf_op jit(solution)/shard_map/all_gather | solution.py:137
  338.3 6.7 %fusion.3 = f32[384,768]{0,1:T(8,128)S(1)} fusion(bf16[4096,768]{1,0:T(8,128)(2,1)} %all-gather.8.cloned.1.call-done, bf16[384,4096]{1,0:T(8,128)(2,1)} %all-gather.6.cloned.1.call-done, f32[4096]{0:T(1024)S(1)} %copy-done.3, f32[384]{0:T(512)S(1)} %add_rsqrt_fusion), kind=kOutput, calls=%fused_computation.6 | convolution fusion | flops 2422210560 | bytes 10634752 | tf_op jit(solution)/shard_map/dot_general | solution.py:135
  345.2 1.1 copy.18
  (32 shorter events, 1.4 us)
Async XLA Ops:
  6.5 201.7 %copy-start = (bf16[1,256,512]{2,1,0:T(8,128)(2,1)S(1)}, bf16[1,256,512]{2,1,0:T(8,128)(2,1)}, u32[]{:S(2)}) copy-start(bf16[1,256,512]{2,1,0:T(8,128)(2,1)} %param.15) | copy-start | bytes 786436
  6.5 94.5 %all-gather.4.cloned.1.call-start = ((), (), s32[]{:S(2)}) async-start(), calls=%async_computation.1 | async-start | bytes 4259840 | tf_op jit(solution)/shard_map/all_gather | solution.py:78
  7.3 174.2 %all-reduce.2.cloned.1.call-start = ((), (), s32[]{:S(2)}) async-start(), calls=%async_computation.2 | async-start | bytes 2097152 | tf_op jit(solution)/shard_map/psum | solution.py:81
  8.7 97.0 %copy-start.4 = (s32[128]{0:T(128)S(1)}, s32[128]{0:T(128)}, u32[]{:S(2)}) copy-start(s32[128]{0:T(128)} %param.19) | copy-start | bytes 1540
  8.7 97.5 %copy-start.1 = (bf16[512,512]{1,0:T(8,128)(2,1)S(1)}, bf16[512,512]{1,0:T(8,128)(2,1)}, u32[]{:S(2)}) copy-start(bf16[512,512]{1,0:T(8,128)(2,1)} %param.12) | copy-start | bytes 1572868
  10.1 171.3 %copy-start.2 = (f32[512]{0:T(512)S(1)}, f32[512]{0:T(512)}, u32[]{:S(2)}) copy-start(f32[512]{0:T(512)} %param.14) | copy-start | bytes 6148
  106.5 231.8 %copy-start.3 = (f32[4096]{0:T(1024)S(1)}, f32[4096]{0:T(1024)}, u32[]{:S(2)}) copy-start(f32[4096]{0:T(1024)} %param.20) | copy-start | bytes 49156
  183.3 24.5 %all-to-all-start = ((bf16[64,2,512]{2,1,0:T(2,128)(2,1)}), bf16[64,2,512]{2,1,0:T(2,128)(2,1)S(1)}, u32[]{:S(2)}, u32[]{:S(2)}) async-start(bf16[64,2,512]{2,1,0:T(2,128)(2,1)} %reshape.199), calls=%async_computation | async-start | bytes 262144 | tf_op jit(solution)/shard_map/all_to_all | solution.py:101
  197.4 52.9 %all-gather.6.cloned.1.call-start = ((), (), s32[]{:S(2)}) async-start(), calls=%async_computation.3 | async-start | bytes 3538944 | tf_op jit(solution)/shard_map/all_gather | solution.py:133
  209.3 129.0 %all-gather.8.cloned.1.call-start = ((), (), s32[]{:S(2)}) async-start(), calls=%async_computation.4 | async-start | bytes 6389760 | tf_op jit(solution)/shard_map/all_gather | solution.py:137
Sparse Core Ops, SparseCore 0:
  10.7 90.2 all-gather.3
  105.8 75.5 all-reduce.1
  209.4 40.8 all-gather.5
  253.5 84.7 all-gather.7
where the time goes:
time: 353 us
  waiting for transfers between devices  298 us (84%)
  between operations  15.2 us (4%)
  starting transfers between devices  14.3 us (4%)
  matrix products  13.8 us (4%)
  other arithmetic  8.27 us (2%)
  local copies, waits for them, and re-layouts  3.69 us (1%)
    all_gather x1, waiting for transfers between devices, shards(): lax.all_gather(out_weight, 'req', axis=1, tiled=True)  91 us
    all_gather x1, waiting for transfers between devices, shards(): lax.all_gather(qkv_weight, 'req', axis=0, tiled=True)  85.4 us
    psum x1, waiting for transfers between devices, shards(): lax.psum(partial_value.astype(jnp.bfloat16), 'tp').astype(jnp.float32)  73.3 us
    all_gather x1, waiting for transfers between devices, shards(): gathered = lax.all_gather(embedded, 'tp', axis=1, tiled=True)  40 us
    all_to_all x1, starting transfers between devices, shards(): lax.all_to_all(outgoing.reshape(requests, capacity, feature_width), 'req'...  14.2 us
  transfers between devices with their start and end apart: 5, of which 5 were waited for; matrix products, arithmetic and copies ran while one was open for 3% of the time, Pallas kernels for 0%

commit v1 on v0

--- a/solution.py
+++ b/solution.py
@@ -6,6 +6,12 @@
 HEAD = 128
 GROUP = 4
 IMG_MAX = 128
+
+
+def summed_here(value, axis):
+    blocks = lax.all_gather(value, axis, axis=0, tiled=False)
+    acc = blocks.sum(axis=0)
+    return acc
 
 
 def request_plan(grid_sizes, image_owner, requests):
@@ -78,7 +84,7 @@
         lax.all_gather(out_weight, "req", axis=1, tiled=True),
         preferred_element_type=jnp.float32,
     )
-    summed = lax.psum(partial_value.astype(jnp.bfloat16), "tp").astype(jnp.float32)
+    summed = summed_here(partial_value.astype(jnp.bfloat16), "tp").astype(jnp.float32)
     own_share = lax.dynamic_slice_in_dim(
         summed, lax.axis_index("tp") * feature_width, feature_width, 1
     )

time: 353 us -> 373 us (1.057)
  waiting for transfers between devices: 298 us -> 317 us
  other arithmetic: 8.27 us -> 12.6 us
  starting transfers between devices: 14.3 us -> 10.5 us
    all_gather x0 -> x1, waiting for transfers between devices: none -> 92.5 us  [summed_here(): blocks = lax.all_gather(value, axis, axis=0, tiled=False)]
    psum x1 -> x0, waiting for transfers between devices: 73.3 us -> none  [shards(): lax.psum(partial_value.astype(jnp.bfloat16), 'tp').astype(jnp.float32)]
    reduce_sum x0 -> x1, other arithmetic: none -> 4.91 us  [summed_here(): acc = blocks.sum(axis=0)]
    all_to_all x1, starting transfers between devices: 14.2 us -> 10.4 us  [shards(): lax.all_to_all(outgoing.reshape(requests, capacity, feature_width), 'req'...]
  transfers between devices with their start and end apart: 5 -> 5, of which waited for: 5 -> 5; matrix products, arithmetic and copies ran while one was open for 3% -> 2% of each run, Pallas kernels for 0% -> 0%
where the time goes in v1:
time: 373 us
  waiting for transfers between devices  317 us (85%)
  between operations  15.3 us (4%)
  matrix products  13.1 us (4%)
  other arithmetic  12.6 us (3%)
  starting transfers between devices  10.5 us (3%)
    all_gather x1, waiting for transfers between devices, summed_here(): blocks = lax.all_gather(value, axis, axis=0, tiled=False)  92.5 us
    all_gather x1, waiting for transfers between devices, shards(): lax.all_gather(out_weight, 'req', axis=1, tiled=True)  91.7 us
    all_gather x1, waiting for transfers between devices, shards(): lax.all_gather(qkv_weight, 'req', axis=0, tiled=True)  85.4 us
    all_gather x1, waiting for transfers between devices, shards(): gathered = lax.all_gather(embedded, 'tp', axis=1, tiled=True)  40.2 us
    all_to_all x1, starting transfers between devices, shards(): lax.all_to_all(outgoing.reshape(requests, capacity, feature_width), 'req'...  10.4 us
  transfers between devices with their start and end apart: 5, of which 5 were waited for; matrix products, arithmetic and copies ran while one was open for 2% of the time, Pallas kernels for 0%

profile of v1, /device:TPU:1, one launch (start us, length us, event | category | flops | bytes accessed | tf_op | source)
XLA Modules:
  0.0 372.5 jit_solution(10457048197082466468)
XLA Ops:
  6.5 0.7 all-gather.6.cloned.1.call-update
  7.3 1.4 reshape.205
  8.7 0.6 reduce_sum.90
  9.3 91.7 %all-gather.6.cloned.1.call-done = bf16[512,4096]{0,1:T(8,128)(2,1)} async-done(((bf16[512,64]{0,1:T(8,128)(2,1)}), bf16[512,4096]{0,1:T(8,128)(2,1)}) %all-gather.6.cloned.1.call-update) | async-done | bytes 4194320 | tf_op jit(solution)/shard_map/all_gather | solution.py:84
  101.1 4.7 %convolution_convert_fusion = bf16[128,4096]{1,0:T(8,128)(2,1)} fusion(bf16[512,4096]{0,1:T(8,128)(2,1)} %all-gather.6.cloned.1.call-done, f32[128,512]{1,0:T(8,128)S(1)} %reduce_sum.90), kind=kOutput, calls=%fused_computation.5 | convolution fusion | flops 537526272 | bytes 5505024 | tf_op jit(solution)/shard_map/dot_general | solution.py:82
  106.3 0.3 reshape.203
  106.6 0.6 reduce_sum.89
  107.4 0.7 fusion.38
  108.2 92.5 %all-gather.12.cloned.1.call-done = bf16[1024,4096]{1,0:T(8,128)(2,1)} async-done(((bf16[128,4096]{1,0:T(8,128)(2,1)}), bf16[1024,4096]{1,0:T(8,128)(2,1)}) %all-gather.12.cloned.1.call-update) | async-done | bytes 8388624 | tf_op jit(solution)/shard_map/all_gather | solution.py:12
  200.7 4.9 %reduce_sum.91 = bf16[128,4096]{1,0:T(8,128)(2,1)S(1)} reduce(bf16[8,128,4096]{2,1,0:T(8,128)(2,1)} %bitcast.17, bf16[]{:T(256)} %constant.69.clone.1), dimensions={0}, to_apply=%region_8.9 | reduce | flops 3670016 | bytes 9437186 | tf_op jit(solution)/shard_map/reduce_sum | solution.py:13
  205.9 0.7 reshape.199
  206.6 10.4 %all-to-all-start = ((bf16[64,2,512]{2,1,0:T(2,128)(2,1)}), bf16[64,2,512]{2,1,0:T(2,128)(2,1)S(1)}, u32[]{:S(2)}, u32[]{:S(2)}) async-start(bf16[64,2,512]{2,1,0:T(2,128)(2,1)} %reshape.199), calls=%async_computation | async-start | bytes 262144 | tf_op jit(solution)/shard_map/all_to_all | solution.py:107
  219.0 0.7 fusion.37
  219.7 1.3 fusion.30
  221.0 6.3 %all-to-all-done = bf16[64,2,512]{2,1,0:T(2,128)(2,1)S(1)} async-done(((bf16[64,2,512]{2,1,0:T(2,128)(2,1)}), bf16[64,2,512]{2,1,0:T(2,128)(2,1)S(1)}, u32[]{:S(2)}, u32[]{:S(2)}) %all-to-all-start) | async-done | bytes 131104 | tf_op jit(solution)/shard_map/all_to_all | solution.py:107
  227.4 0.3 fusion.14
  227.7 1.1 fusion.7
  228.9 0.5 all-gather.10.cloned.1.call-update
  229.4 0.4 fusion.21
  229.8 40.2 %all-gather.8.cloned.1.call-done = bf16[384,4096]{1,0:T(8,128)(2,1)} async-done(((bf16[384,512]{1,0:T(8,128)(2,1)}), bf16[384,4096]{1,0:T(8,128)(2,1)}) %all-gather.8.cloned.1.call-update) | async-done | bytes 3145744 | tf_op jit(solution)/shard_map/all_gather | solution.py:139
  270.0 2.6 fusion
  272.6 85.4 %all-gather.10.cloned.1.call-done = bf16[4096,768]{1,0:T(8,128)(2,1)} async-done(((bf16[64,768]{1,0:T(8,128)(2,1)}), bf16[4096,768]{1,0:T(8,128)(2,1)}) %all-gather.10.cloned.1.call-update) | async-done | bytes 6291472 | tf_op jit(solution)/shard_map/all_gather | solution.py:143
  358.0 6.7 %fusion.3 = f32[384,768]{0,1:T(8,128)S(1)} fusion(bf16[4096,768]{1,0:T(8,128)(2,1)} %all-gather.10.cloned.1.call-done, bf16[384,4096]{1,0:T(8,128)(2,1)} %all-gather.8.cloned.1.call-done, f32[4096]{0:T(1024)S(1)} %copy-done.3, f32[384]{0:T(512)S(1)} %add_rsqrt_fusion), kind=kOutput, calls=%fused_computation.6 | convolution fusion | flops 2422210560 | bytes 10634752 | tf_op jit(solution)/shard_map/dot_general | solution.py:141
  364.9 1.1 copy.18
  (35 shorter events, 1.3 us)
Async XLA Ops:
  6.5 221.2 %copy-start = (bf16[1,256,512]{2,1,0:T(8,128)(2,1)S(1)}, bf16[1,256,512]{2,1,0:T(8,128)(2,1)}, u32[]{:S(2)}) copy-start(bf16[1,256,512]{2,1,0:T(8,128)(2,1)} %param.15) | copy-start | bytes 786436
  6.5 94.5 %all-gather.6.cloned.1.call-start = ((), (), s32[]{:S(2)}) async-start(), calls=%async_computation.1 | async-start | bytes 4259840 | tf_op jit(solution)/shard_map/all_gather | solution.py:84
  7.3 193.4 %all-gather.12.cloned.1.call-start = ((), (), s32[]{:S(2)}) async-start(), calls=%async_computation.4 | async-start | bytes 9437184 | tf_op jit(solution)/shard_map/all_gather | solution.py:12
  8.7 97.1 %copy-start.4 = (s32[128,2]{0,1:T(2,128)S(1)}, s32[128,2]{0,1:T(2,128)}, u32[]{:S(2)}) copy-start(s32[128,2]{0,1:T(2,128)} %param.18) | copy-start | bytes 3076
  8.7 97.1 %copy-start.5 = (s32[128]{0:T(128)S(1)}, s32[128]{0:T(128)}, u32[]{:S(2)}) copy-start(s32[128]{0:T(128)} %param.19) | copy-start | bytes 1540
  8.7 97.6 %copy-start.1 = (bf16[512,512]{1,0:T(8,128)(2,1)S(1)}, bf16[512,512]{1,0:T(8,128)(2,1)}, u32[]{:S(2)}) copy-start(bf16[512,512]{1,0:T(8,128)(2,1)} %param.12) | copy-start | bytes 1572868
  200.7 4.9 %copy-start.2 = (f32[512]{0:T(512)S(1)}, f32[512]{0:T(512)}, u32[]{:S(2)}) copy-start(f32[512]{0:T(512)} %param.14) | copy-start | bytes 6148
  205.6 152.3 %copy-start.3 = (f32[4096]{0:T(1024)S(1)}, f32[4096]{0:T(1024)}, u32[]{:S(2)}) copy-start(f32[4096]{0:T(1024)} %param.20) | copy-start | bytes 49156
  206.6 20.8 %all-to-all-start = ((bf16[64,2,512]{2,1,0:T(2,128)(2,1)}), bf16[64,2,512]{2,1,0:T(2,128)(2,1)S(1)}, u32[]{:S(2)}, u32[]{:S(2)}) async-start(bf16[64,2,512]{2,1,0:T(2,128)(2,1)} %reshape.199), calls=%async_computation | async-start | bytes 262144 | tf_op jit(solution)/shard_map/all_to_all | solution.py:107
  217.0 53.0 %all-gather.8.cloned.1.call-start = ((), (), s32[]{:S(2)}) async-start(), calls=%async_computation.2 | async-start | bytes 3538944 | tf_op jit(solution)/shard_map/all_gather | solution.py:139
  228.8 129.1 %all-gather.10.cloned.1.call-start = ((), (), s32[]{:S(2)}) async-start(), calls=%async_computation.3 | async-start | bytes 6389760 | tf_op jit(solution)/shard_map/all_gather | solution.py:143
Sparse Core Ops, SparseCore 0:
  10.7 90.2 all-gather.5
  105.9 94.7 all-gather.11
  228.9 41.0 all-gather.7
  273.2 84.7 all-gather.9
